TPU v7x, 32 devices: a whole 2x2x4 slice. The times are simulated.
32 devices in a mesh: groups: 2 (over x), dp: 4 (over y, core), hidden: 4 (over z).
Axes of the slice: x: 2, y: 2, z: 4, core: 2. Of those that a mesh axis runs over, the one named last changes fastest.
Arguments:
- activations: bfloat16 [24576, 8192], P(('groups', 'dp'), 'hidden'), parts along dimension 0, may hold values from -6 to 6
- cotangent: bfloat16 [24576, 8192], P(('groups', 'dp'), 'hidden'), parts along dimension 0
- up_factor_matrix: bfloat16 [8192, 64], P('hidden'), may hold values from -0.0625 to 0.0625
- input_sketch: bfloat16 [8192, 128], P('hidden'), may hold values from -0.0625 to 0.0625
- rank_sketch: float32 [64, 32], replicated, may hold values from -0.75 to 0.75
Outputs:
- features: bfloat16 [48, 4096], P(('groups', 'dp'), 'hidden'), parts along dimension 0
- scores: float32 [48, 24], P(('groups', 'dp'), 'hidden'), parts along dimension 0
There are 2 independent parts, one for each index of `groups`. A program takes and returns all parts, laid end to end along the dimension named above; an argument that names none is the same for every part. Nothing has to cross between parts.
All inputs are finite; a program needn't handle non-finite values.
Results may differ from a plain program's by a relative error of at most 0.0017.
Values may be sent and summed in bfloat16 or wider, within the bound.
No kernel may reach another device: no remote copies, remote signals or barrier semaphores. Data moves between devices by JAX's collectives and lax.ppermute only.
A program may use at most 64 MiB of HBM per device.

v0:
```python
import math
import jax
import jax.numpy as jnp
from jax import lax
from jax.sharding import PartitionSpec as P

SEQ = 512
epsilon = 1e-05
HI = lax.Precision.HIGHEST


def partial_features(activations, cotangent, up_factor_matrix, input_sketch, rank_sketch):
    examples = activations.shape[0] // SEQ
    backward_pass = jnp.dot(cotangent, up_factor_matrix, preferred_element_type=jnp.float32)
    rank_part = jnp.dot(backward_pass, rank_sketch, precision=HI)
    rank_full = lax.psum(rank_part, "hidden")
    input_part = jnp.dot(activations, input_sketch, preferred_element_type=jnp.float32)
    rank_rows = rank_full.reshape(examples, SEQ, rank_full.shape[1])
    input_rows = input_part.reshape(examples, SEQ, input_part.shape[1])
    return jnp.einsum("esa,esb->eab", rank_rows, input_rows, precision=HI)


def per_device(activations, cotangent, up_factor_matrix, input_sketch, rank_sketch):
    examples = activations.shape[0] // SEQ
    partial = partial_features(activations, cotangent, up_factor_matrix, input_sketch, rank_sketch)
    own = lax.psum_scatter(partial, "hidden", scatter_dimension=1, tiled=True)
    features = own.reshape(examples, -1).astype(jnp.bfloat16)
    widened = features.astype(jnp.float32)
    every = lax.all_gather(features, "dp", axis=0, tiled=True).astype(jnp.float32)
    all_count = every.shape[0]
    weight = 1.0 / (jnp.sum(every * every, axis=0) / all_count + epsilon)
    partial_scores = jnp.dot(widened * weight, every.T, precision=HI)
    feat_total = features.shape[1] * lax.axis_size("hidden")
    scores = lax.psum_scatter(
        partial_scores / math.sqrt(feat_total), "hidden", scatter_dimension=1, tiled=True
    )
    return (features, scores)


def solution(mesh):
    placed = (
        P(("groups", "dp"), "hidden"),
        P(("groups", "dp"), "hidden"),
        P("hidden", None),
        P("hidden", None),
        P(),
    )
    return jax.shard_map(
        per_device,
        mesh=mesh,
        in_specs=placed,
        out_specs=(P(("groups", "dp"), "hidden"), P(("groups", "dp"), "hidden")),
        check_vma=False,
    )
```

profile of v0, /device:TPU:0, one launch (start us, length us, event | category | flops | bytes accessed | tf_op | source)
XLA Modules:
  0.0 102.2 jit_solution(1430355380435664496)
XLA Ops:
  7.2 0.0 copy-start
  7.2 0.0 copy-start.2
  7.2 0.0 all-reduce.3.cloned.1.call-start
  7.2 8.5 %fusion.3 = f32[3072,64]{0,1:T(8,128)S(1)} fusion(bf16[3072,2048]{1,0:T(8,128)(2,1)} %param.6, bf16[2048,64]{0,1:T(8,128)(2,1)} %param.7), kind=kOutput, calls=%fused_computation.9 | convolution fusion | flops 805306368 | bytes 13631488 | tf_op jit(solution)/shard_map/dot_general | solution.py:14
  15.8 0.0 copy-done.2
  15.8 0.0 copy-start.3
  15.8 0.6 fusion.4
  16.4 0.8 copy.16
  17.1 0.0 all-reduce.3.cloned.1.call-update
  17.2 0.0 reduce-scatter.3.cloned.1.call-start
  17.2 0.0 copy-done
  17.2 6.4 %fusion.5 = f32[3072,128]{1,0:T(8,128)S(1)} fusion(bf16[3072,2048]{1,0:T(8,128)(2,1)} %param.5, bf16[2048,128]{1,0:T(8,128)(2,1)S(1)} %copy-done), kind=kOutput, calls=%fused_computation.11 | convolution fusion | flops 1610612736 | bytes 14680064 | tf_op jit(solution)/shard_map/dot_general | solution.py:17
  23.7 33.3 %all-reduce.3.cloned.1.call-done = f32[6,512,32]{1,2,0:T(8,128)} async-done(((f32[6,512,32]{1,2,0:T(8,128)}), f32[6,512,32]{1,2,0:T(8,128)}) %all-reduce.3.cloned.1.call-update) | async-done | bytes 393232 | tf_op jit(solution)/shard_map/psum | solution.py:16
  57.0 2.6 %fusion.6 = f32[6,32,128]{2,1,0:T(8,128)} fusion(f32[6,512,32]{1,2,0:T(8,128)} %all-reduce.3.cloned.1.call-done, f32[6,512,128]{2,1,0:T(8,128)S(1)} %bitcast.23), kind=kOutput, calls=%fused_computation.12 | convolution fusion | flops 150994944 | bytes 2064384 | tf_op jit(solution)/shard_map/esa,esb->eab/dot_general | solution.py:20
  59.5 0.0 reduce-scatter.3.cloned.1.call-update
  59.6 0.0 copy-done.3
  59.6 0.6 dynamic-slice
  60.8 18.0 %reduce-scatter.3.cloned.1.call-done = f32[6,8,128]{2,1,0:T(8,128)} async-done(((f32[6,32,128]{2,1,0:T(8,128)}), f32[6,8,128]{2,1,0:T(8,128)}) %reduce-scatter.3.cloned.1.call-update) | async-done | bytes 24592 | tf_op jit(solution)/shard_map/reduce_scatter | solution.py:26
  78.9 0.7 convert_element_type.12
  79.6 5.2 %all-gather = bf16[4,6,1024]{2,1,0:T(8,128)(2,1)S(1)} all-gather(bf16[1,6,1024]{2,1,0:T(8,128)(2,1)S(1)} %reshape.19), channel_id=1, replica_groups=mesh['groups'=2,'dp'=4,'hidden'=4] {'dp'}, dimensions={0}, use_global_device_ids=true | all-gather | bytes 61440 | tf_op jit(solution)/shard_map/all_gather | solution.py:29
  84.9 0.7 convert_bitcast_fusion
  85.7 0.0 copy-start.1
  85.7 0.1 convolution_multiply_fusion
  85.8 8.9 %all-reduce = f32[6,24]{1,0:T(8,128)S(1)} all-reduce(f32[6,24]{1,0:T(8,128)S(1)} %convolution_multiply_fusion), channel_id=3, replica_groups=mesh['groups'=2,'dp'=4,'hidden'=4] {'hidden'}, use_global_device_ids=true, to_apply=%region_3.0.clone | all-reduce | flops 144 | bytes 1152
  94.7 0.7 constant_dynamic-slice_fusion
  95.4 0.0 copy-done.1
  (5 shorter events, 0.1 us)
Async XLA Ops:
  7.2 10.0 %copy-start = (bf16[2048,128]{1,0:T(8,128)(2,1)S(1)}, bf16[2048,128]{1,0:T(8,128)(2,1)}, u32[]{:S(2)}) copy-start(bf16[2048,128]{1,0:T(8,128)(2,1)} %param.8) | copy-start | bytes 1572868
  7.2 8.6 %copy-start.2 = (f32[64,32]{0,1:T(8,128)S(1)}, f32[64,32]{0,1:T(8,128)}, u32[]{:S(2)}) copy-start(f32[64,32]{0,1:T(8,128)} %param.9) | copy-start | bytes 24580
  7.2 49.8 %all-reduce.3.cloned.1.call-start = ((), (), s32[]{:S(2)}) async-start(), calls=%async_computation.1 | async-start | bytes 786432 | tf_op jit(solution)/shard_map/psum | solution.py:16
  15.8 43.8 %copy-start.3 = (u32[32]{0:T(128)S(1)}, u32[32]{0:T(128)}, u32[]{:S(2)}) copy-start(u32[32]{0:T(128)} %constant.14) | copy-start | bytes 388
  17.2 61.7 %reduce-scatter.3.cloned.1.call-start = ((), (), s32[]{:S(2)}) async-start(), calls=%async_computation.2 | async-start | bytes 122880 | tf_op jit(solution)/shard_map/reduce_scatter | solution.py:26
  85.7 9.7 %copy-start.1 = (bf16[1,6,8,128]{3,1,2,0:T(8,128)(2,1)}, bf16[1,6,8,128]{3,1,2,0:T(8,128)(2,1)S(1)}, u32[]{:S(2)}) copy-start(bf16[1,6,8,128]{3,1,2,0:T(8,128)(2,1)S(1)} %copy.17) | copy-start | bytes 36868
Sparse Core Ops, SparseCore 0:
  17.3 39.6 all-reduce.2
  59.7 19.1 reduce-scatter.2
where the time goes:
time: 103 us; the launch traced here: 102 us
  waiting for transfers between devices  51.4 us (50%)
  matrix products  18.2 us (18%)
  between operations  14.8 us (14%)
  blocking collectives  14.1 us (14%)
  local copies, waits for them, and re-layouts  2.12 us (2%)
  other arithmetic  1.51 us (1%)
    psum x1, waiting for transfers between devices, partial_features(): rank_full = lax.psum(rank_part, 'hidden')  33.3 us
    reduce_scatter x1, waiting for transfers between devices, per_device(): own = lax.psum_scatter(partial, 'hidden', scatter_dimension=1, tiled=True)  18 us
    unnamed x1, blocking collectives  8.87 us
    dot_general x1, matrix products, partial_features(): jnp.dot(cotangent, up_factor_matrix, preferred_element_type=jnp.float32)  8.54 us
    dot_general x1, matrix products, partial_features(): jnp.dot(activations, input_sketch, preferred_element_type=jnp.float32)  6.43 us
    all_gather x1, blocking collectives, per_device(): lax.all_gather(features, 'dp', axis=0, tiled=True).astype(jnp.float32)  5.24 us
    dot_general x1, matrix products, partial_features(): return jnp.einsum('esa,esb->eab', rank_rows, input_rows, precision=HI)  2.56 us
  transfers between devices with their start and end apart: 2, of which 2 were waited for; matrix products, arithmetic and copies ran while one was open for 7% of the time, Pallas kernels for 0%

commit v1 on v0

--- a/solution.py
+++ b/solution.py
@@ -13,7 +13,15 @@
     examples = activations.shape[0] // SEQ
     backward_pass = jnp.dot(cotangent, up_factor_matrix, preferred_element_type=jnp.float32)
     rank_part = jnp.dot(backward_pass, rank_sketch, precision=HI)
-    rank_full = lax.psum(rank_part, "hidden")
+    workers = lax.axis_size("hidden")
+    rank_full = rank_part
+    for jj in [dev_j for dev_j in (1, 2, 4, 8, 16) if dev_j < workers]:
+        history = []
+        ii = 0
+        while ii < workers:
+            history.append((ii, ii ^ jj))
+            ii += 1
+        rank_full = rank_full + lax.ppermute(rank_full, "hidden", history)
     input_part = jnp.dot(activations, input_sketch, preferred_element_type=jnp.float32)
     rank_rows = rank_full.reshape(examples, SEQ, rank_full.shape[1])
     input_rows = input_part.reshape(examples, SEQ, input_part.shape[1])

time: 103 us -> 94.3 us (0.916)
  waiting for transfers between devices: 51.4 us -> 41.8 us
  starting transfers between devices: 0.08 us -> 5.97 us
  matrix products: 18.2 us -> 14.3 us
    psum x1 -> x0, waiting for transfers between devices: 33.3 us -> none  [partial_features(): rank_full = lax.psum(rank_part, 'hidden')]
    ppermute x0 -> x2, waiting for transfers between devices: none -> 22.5 us  [partial_features(): rank_full = rank_full + lax.ppermute(rank_full, 'hidden', history)]
    ppermute x0 -> x2, starting transfers between devices: none -> 5.94 us  [partial_features(): rank_full = rank_full + lax.ppermute(rank_full, 'hidden', history)]
    dot_general x1, matrix products: 6.43 us -> 3.43 us  [partial_features(): jnp.dot(activations, input_sketch, preferred_element_type=jnp.float32)]
    reduce_scatter x1, waiting for transfers between devices: 18 us -> 19.3 us  [per_device(): own = lax.psum_scatter(partial, 'hidden', scatter_dimension=1, tiled=True)]
  transfers between devices with their start and end apart: 2 -> 3, of which waited for: 2 -> 3; matrix products, arithmetic and copies ran while one was open for 7% -> 4% of each run, Pallas kernels for 0% -> 0%
where the time goes in v1:
time: 94.3 us; the launch traced here: 94 us
  waiting for transfers between devices  41.8 us (44%)
  between operations  14.8 us (16%)
  matrix products  14.3 us (15%)
  blocking collectives  14.2 us (15%)
  starting transfers between devices  5.97 us (6%)
  other arithmetic  1.59 us (2%)
  local copies, waits for them, and re-layouts  1.35 us (1%)
    ppermute x2, waiting for transfers between devices, partial_features(): rank_full = rank_full + lax.ppermute(rank_full, 'hidden', history)  22.5 us
    reduce_scatter x1, waiting for transfers between devices, per_device(): own = lax.psum_scatter(partial, 'hidden', scatter_dimension=1, tiled=True)  19.3 us
    unnamed x1, blocking collectives  8.93 us
    dot_general x1, matrix products, partial_features(): jnp.dot(cotangent, up_factor_matrix, preferred_element_type=jnp.float32)  8.64 us
    ppermute x2, starting transfers between devices, partial_features(): rank_full = rank_full + lax.ppermute(rank_full, 'hidden', history)  5.94 us
    all_gather x1, blocking collectives, per_device(): lax.all_gather(features, 'dp', axis=0, tiled=True).astype(jnp.float32)  5.24 us
    dot_general x1, matrix products, partial_features(): jnp.dot(activations, input_sketch, preferred_element_type=jnp.float32)  3.43 us
  transfers between devices with their start and end apart: 3, of which 3 were waited for; matrix products, arithmetic and copies ran while one was open for 4% of the time, Pallas kernels for 0%

profile of v1, /device:TPU:0, one launch (start us, length us, event | category | flops | bytes accessed | tf_op | source)
XLA Modules:
  0.0 94.0 jit_solution(14600837359801776262)
XLA Ops:
  7.2 0.0 copy-start
  7.2 0.0 copy-start.2
  7.2 0.0 reduce-scatter.3.cloned.1.call-start
  7.2 0.0 copy-start.3
  7.2 8.6 %fusion.6 = f32[3072,64]{0,1:T(8,128)S(1)} fusion(bf16[3072,2048]{1,0:T(8,128)(2,1)} %param.6, bf16[2048,64]{0,1:T(8,128)(2,1)} %param.7), kind=kOutput, calls=%fused_computation.11 | convolution fusion | flops 805306368 | bytes 13631488 | tf_op jit(solution)/shard_map/dot_general | solution.py:14
  15.9 0.0 copy-done.2
  15.9 0.0 copy-start.4
  15.9 0.6 fusion.7
  16.5 3.1 %collective-permute-start = (f32[3072,32]{0,1:T(8,128)S(1)}, f32[3072,32]{0,1:T(8,128)S(1)}, u32[]{:S(2)}, u32[]{:S(2)}) collective-permute-start(f32[3072,32]{0,1:T(8,128)S(1)} %fusion.7), channel_id=1, source_target_pairs={{0,1},{1,0},{2,3},{3,2},{4,5},{5,4},{6,7},{7,6},{8,9},{9,8},{10,11... | collective-permute-start | bytes 1179656 | tf_op jit(solution)/shard_map/ppermute | solution.py:24
  19.6 9.1 %collective-permute-done = f32[3072,32]{0,1:T(8,128)S(1)} collective-permute-done((f32[3072,32]{0,1:T(8,128)S(1)}, f32[3072,32]{0,1:T(8,128)S(1)}, u32[]{:S(2)}, u32[]{:S(2)}) %collective-permute-start) | collective-permute-done | bytes 393248 | tf_op jit(solution)/shard_map/ppermute | solution.py:24
  28.7 2.8 %collective-permute-start.1 = (f32[3072,32]{0,1:T(8,128)S(1)}, f32[3072,32]{0,1:T(8,128)S(1)}, u32[]{:S(2)}, u32[]{:S(2)}) collective-permute-start(f32[3072,32]{0,1:T(8,128)S(1)} %add.20), channel_id=1, source_target_pairs={{0,2},{1,3},{2,0},{3,1},{4,6},{5,7},{6,4},{7,5},{8,10},{9,11},{10,... | collective-permute-start | bytes 1179656 | tf_op jit(solution)/shard_map/ppermute | solution.py:24
  31.6 0.0 copy-done
  31.6 0.0 copy-done.3
  31.6 3.4 %fusion.8 = f32[3072,128]{1,0:T(8,128)S(1)} fusion(bf16[3072,2048]{1,0:T(8,128)(2,1)S(1)} %copy-done.3, bf16[2048,128]{1,0:T(8,128)(2,1)S(1)} %copy-done), kind=kOutput, calls=%fused_computation.13 | convolution fusion | flops 1610612736 | bytes 14680064 | tf_op jit(solution)/shard_map/dot_general | solution.py:25
  35.0 13.4 %collective-permute-done.1 = f32[3072,32]{0,1:T(8,128)S(1)} collective-permute-done((f32[3072,32]{0,1:T(8,128)S(1)}, f32[3072,32]{0,1:T(8,128)S(1)}, u32[]{:S(2)}, u32[]{:S(2)}) %collective-permute-start.1) | collective-permute-done | bytes 393248 | tf_op jit(solution)/shard_map/ppermute | solution.py:24
  48.5 1.6 %fusion = f32[6,32,128]{2,1,0:T(8,128)} fusion(f32[6,512,128]{2,1,0:T(8,128)S(1)} %bitcast.21, f32[4,6,8,512]{3,2,1,0:T(8,128)S(1)} %bitcast.22), kind=kOutput, calls=%fused_computation.1 | convolution fusion | flops 150994944 | bytes 2064384 | tf_op jit(solution)/shard_map/esa,esb->eab/dot_general | solution.py:28
  50.0 0.0 reduce-scatter.3.cloned.1.call-update
  50.0 0.0 copy-done.4
  50.1 0.6 dynamic-slice
  51.3 19.3 %reduce-scatter.3.cloned.1.call-done = f32[6,8,128]{2,1,0:T(8,128)} async-done(((f32[6,32,128]{2,1,0:T(8,128)}), f32[6,8,128]{2,1,0:T(8,128)}) %reduce-scatter.3.cloned.1.call-update) | async-done | bytes 24592 | tf_op jit(solution)/shard_map/reduce_scatter | solution.py:34
  70.6 0.7 convert_element_type.12
  71.3 5.2 %all-gather = bf16[4,6,1024]{2,1,0:T(8,128)(2,1)S(1)} all-gather(bf16[1,6,1024]{2,1,0:T(8,128)(2,1)S(1)} %reshape.19), channel_id=1, replica_groups=mesh['groups'=2,'dp'=4,'hidden'=4] {'dp'}, dimensions={0}, use_global_device_ids=true | all-gather | bytes 61440 | tf_op jit(solution)/shard_map/all_gather | solution.py:37
  76.7 0.7 convert_bitcast_fusion
  77.4 0.0 copy-start.1
  77.4 0.1 convolution_multiply_fusion
  77.5 8.9 %all-reduce = f32[6,24]{1,0:T(8,128)S(1)} all-reduce(f32[6,24]{1,0:T(8,128)S(1)} %convolution_multiply_fusion), channel_id=3, replica_groups=mesh['groups'=2,'dp'=4,'hidden'=4] {'hidden'}, use_global_device_ids=true, to_apply=%region_2.0.clone | all-reduce | flops 144 | bytes 1152
  86.5 0.7 constant_dynamic-slice_fusion
  87.1 0.0 copy-done.1
  (7 shorter events, 0.2 us)
Async XLA Ops:
  7.2 24.4 %copy-start = (bf16[2048,128]{1,0:T(8,128)(2,1)S(1)}, bf16[2048,128]{1,0:T(8,128)(2,1)}, u32[]{:S(2)}) copy-start(bf16[2048,128]{1,0:T(8,128)(2,1)} %param.8) | copy-start | bytes 1572868
  7.2 8.7 %copy-start.2 = (f32[64,32]{0,1:T(8,128)S(1)}, f32[64,32]{0,1:T(8,128)}, u32[]{:S(2)}) copy-start(f32[64,32]{0,1:T(8,128)} %param.9) | copy-start | bytes 24580
  7.2 63.4 %reduce-scatter.3.cloned.1.call-start = ((), (), s32[]{:S(2)}) async-start(), calls=%async_computation.1 | async-start | bytes 122880 | tf_op jit(solution)/shard_map/reduce_scatter | solution.py:34
  7.2 24.3 %copy-start.3 = (bf16[3072,2048]{1,0:T(8,128)(2,1)S(1)}, bf16[3072,2048]{1,0:T(8,128)(2,1)}, u32[]{:S(2)}) copy-start(bf16[3072,2048]{1,0:T(8,128)(2,1)} %param.5) | copy-start | bytes 37748740
  15.9 34.2 %copy-start.4 = (u32[32]{0:T(128)S(1)}, u32[32]{0:T(128)}, u32[]{:S(2)}) copy-start(u32[32]{0:T(128)} %constant.14) | copy-start | bytes 388
  16.5 12.2 %collective-permute-start = (f32[3072,32]{0,1:T(8,128)S(1)}, f32[3072,32]{0,1:T(8,128)S(1)}, u32[]{:S(2)}, u32[]{:S(2)}) collective-permute-start(f32[3072,32]{0,1:T(8,128)S(1)} %fusion.7), channel_id=1, source_target_pairs={{0,1},{1,0},{2,3},{3,2},{4,5},{5,4},{6,7},{7,6},{8,9},{9,8},{10,11... | collective-permute-start | bytes 1179656 | tf_op jit(solution)/shard_map/ppermute | solution.py:24
  28.7 19.7 %collective-permute-start.1 = (f32[3072,32]{0,1:T(8,128)S(1)}, f32[3072,32]{0,1:T(8,128)S(1)}, u32[]{:S(2)}, u32[]{:S(2)}) collective-permute-start(f32[3072,32]{0,1:T(8,128)S(1)} %add.20), channel_id=1, source_target_pairs={{0,2},{1,3},{2,0},{3,1},{4,6},{5,7},{6,4},{7,5},{8,10},{9,11},{10,... | collective-permute-start | bytes 1179656 | tf_op jit(solution)/shard_map/ppermute | solution.py:24
  77.4 9.7 %copy-start.1 = (bf16[1,6,8,128]{3,1,2,0:T(8,128)(2,1)}, bf16[1,6,8,128]{3,1,2,0:T(8,128)(2,1)S(1)}, u32[]{:S(2)}) copy-start(bf16[1,6,8,128]{3,1,2,0:T(8,128)(2,1)S(1)} %copy.19) | copy-start | bytes 36868
Sparse Core Ops, SparseCore 0:
  50.2 20.3 reduce-scatter.2
